TPU v7x, 256 devices: a whole 4x4x8 slice. The times are simulated.
256 devices in a mesh: segment: 2 (over y_hi), blk: 32 (over z, x), mp: 4 (over y_lo, core).
Axes of the slice: x: 4, y: 4 (y_hi: 2, y_lo: 2; y = y_hi * 2 + y_lo), z: 8, core: 2. Of those that a mesh axis runs over, the one named last changes fastest.
Arguments:
- section_input: bfloat16 [2, 8192, 1536], P('segment', 'blk', 'mp'), may hold values from -36 to 36
- row_code: int32 [2, 8192], P('segment', 'blk'), may hold values from 0 to 255
- code_table: bfloat16 [2, 256, 1536], P('segment', None, 'mp'), may hold values from -6 to 6
- self_gain: float32 [2, 1536], P('segment'), may hold values from 0.1 to 1.9
- self_weights: bfloat16 [2, 3, 1536, 1536], P('segment', None, None, 'mp'), may hold values from -0.22963966 to 0.22963966
- self_out: bfloat16 [2, 1536, 1536], P('segment', 'mp'), may hold values from -0.15625 to 0.15625
- cross_gain: float32 [1536], replicated, may hold values from 0.1 to 1.9
- memory_gain: float32 [1536], replicated, may hold values from 0.1 to 1.9
- cross_weights: bfloat16 [3, 1536, 1536], P(None, None, 'mp'), may hold values from -0.22963966 to 0.22963966
- cross_out: bfloat16 [1536, 1536], P('mp'), may hold values from -0.15625 to 0.15625
Outputs:
- sections: bfloat16 [2, 8192, 1536], P('segment', 'blk', 'mp')
All inputs are finite; a program needn't handle non-finite values.
Results may differ from a plain program's by a relative error of at most 0.0085.
Values may be sent and summed in bfloat16 or wider, within the bound.
No kernel may reach another device: no remote copies, remote signals or barrier semaphores. Data moves between devices by JAX's collectives and lax.ppermute only.
A program may use at most 128 MiB of HBM per device.

v0:
```python
import math
import jax
import jax.numpy as jnp
from jax import lax
from jax.sharding import PartitionSpec as P

HEAD_DIM = 128


def shifted(value, axis, steps):
    count = lax.axis_size(axis)
    initial, last = (max(0, -steps), min(count, count - steps))
    return lax.ppermute(value, axis, [(source, source + steps) for source in range(initial, last)])


def rms_norm(values, gain):
    widened = values.astype(jnp.float32)
    meansq = jnp.mean(widened * widened, axis=-1, keepdims=True)
    return (widened * lax.rsqrt(meansq + 1e-05) * gain).astype(jnp.bfloat16)


def project(normed, weight):
    return jnp.dot(normed, weight, preferred_element_type=jnp.float32).astype(jnp.bfloat16)


def make_fold(queries):
    row_count = queries.shape[0]
    head_count = queries.shape[1] // HEAD_DIM
    grouped = queries.reshape(row_count, head_count, HEAD_DIM)
    factor = 1.0 / math.sqrt(HEAD_DIM)

    def fold(running, piece, start):
        piece_rows = piece.shape[1]
        block_rows = math.gcd(piece_rows, 1024)
        key_blocks = piece[0].reshape(piece_rows // block_rows, block_rows, head_count, HEAD_DIM)
        value_blocks = piece[1].reshape(piece_rows // block_rows, block_rows, head_count, HEAD_DIM)

        def absorb(current, blocks):
            running_max, running_sum, running_out = current
            key_block, value_block = blocks
            scores = (
                jnp.einsum("qhd,khd->qhk", grouped, key_block, preferred_element_type=jnp.float32)
                * factor
            )
            new_max = jnp.maximum(running_max, jnp.max(scores, axis=2))
            shrink = jnp.exp(running_max - new_max)
            weights = jnp.exp(scores - new_max[:, :, None])
            new_sum = running_sum * shrink + jnp.sum(weights, axis=2)
            new_out = running_out * shrink[:, :, None] + jnp.einsum(
                "qhk,khd->qhd",
                weights.astype(jnp.bfloat16),
                value_block,
                preferred_element_type=jnp.float32,
            )
            return ((new_max, new_sum, new_out), None)

        result, unused = lax.scan(absorb, running, (key_blocks, value_blocks))
        return result

    start_state = (
        jnp.full((row_count, head_count), -1e30, jnp.float32),
        jnp.zeros((row_count, head_count), jnp.float32),
        jnp.zeros((row_count, head_count, HEAD_DIM), jnp.float32),
    )
    return (fold, start_state)


def finish(running):
    running_max, running_sum, running_out = running
    merged = running_out / running_sum[:, :, None]
    return merged.reshape(merged.shape[0], merged.shape[1] * merged.shape[2]).astype(jnp.bfloat16)


def memory_projection(memory_full, memory_gain, cross_weights):
    memory_normed = rms_norm(memory_full, memory_gain)
    return jnp.stack(
        [project(memory_normed, cross_weights[1]), project(memory_normed, cross_weights[2])]
    )


def on_device(
    section_input,
    row_code,
    code_table,
    self_gain,
    self_weights,
    self_out,
    cross_gain,
    memory_gain,
    cross_weights,
    cross_out,
):
    local_rows = section_input.shape[1]
    codes_total = code_table.shape[1]
    matches = (
        row_code[0][:, None] == lax.broadcasted_iota(jnp.int32, (local_rows, codes_total), 1)
    ).astype(jnp.bfloat16)
    looked = jnp.dot(matches, code_table[0], preferred_element_type=jnp.float32)
    embedded = (section_input[0].astype(jnp.float32) + looked).astype(jnp.bfloat16)
    embedded_full = lax.all_gather(embedded, "mp", axis=1, tiled=True)
    normed = rms_norm(embedded_full, self_gain[0])
    self_queries = project(normed, self_weights[0, 0])
    self_pairs = jnp.stack(
        [project(normed, self_weights[0, 1]), project(normed, self_weights[0, 2])]
    )
    fold_self, self_start = make_fold(self_queries)
    self_running = fold_self(
        self_start, lax.all_gather(self_pairs, "blk", axis=1, tiled=True), jnp.int32(0)
    )
    partial_out = jnp.dot(finish(self_running), self_out[0], preferred_element_type=jnp.float32)
    reduced = lax.psum_scatter(
        partial_out.astype(jnp.bfloat16), "mp", scatter_dimension=1, tiled=True
    ).astype(jnp.float32)
    hidden_part = (embedded.astype(jnp.float32) + reduced).astype(jnp.bfloat16)
    hidden_full = lax.all_gather(hidden_part, "mp", axis=1, tiled=True)
    cross_queries = project(rms_norm(hidden_full, cross_gain), cross_weights[0])
    fold_cross, cross_start = make_fold(cross_queries)
    arrived = shifted(hidden_part, "segment", 1)
    memory_full = lax.all_gather(arrived, "mp", axis=1, tiled=True)
    memory_pairs = memory_projection(memory_full, memory_gain, cross_weights)
    crossed = fold_cross(
        cross_start, lax.all_gather(memory_pairs, "blk", axis=1, tiled=True), jnp.int32(0)
    )
    cross_partial = jnp.dot(finish(crossed), cross_out, preferred_element_type=jnp.float32)
    cross_reduced = lax.psum_scatter(
        cross_partial.astype(jnp.bfloat16), "mp", scatter_dimension=1, tiled=True
    ).astype(jnp.float32)
    decoded = (hidden_part.astype(jnp.float32) + cross_reduced).astype(jnp.bfloat16)
    chosen = jnp.where(lax.axis_index("segment") == 0, hidden_part, decoded)
    return chosen[None]


def solution(mesh):
    return jax.shard_map(
        on_device,
        mesh=mesh,
        in_specs=(
            P("segment", "blk", "mp"),
            P("segment", "blk"),
            P("segment", None, "mp"),
            P("segment", None),
            P("segment", None, None, "mp"),
            P("segment", "mp", None),
            P(),
            P(),
            P(None, None, "mp"),
            P("mp", None),
        ),
        out_specs=P("segment", "blk", "mp"),
        check_vma=False,
    )
```

profile of v0, /device:TPU:1, one launch (start us, length us, event | category | flops | bytes accessed | tf_op | source)
XLA Modules:
  0.0 598.6 jit_solution(17165010562332060110)
XLA Ops:
  8.0 10.3 %all_gather.15 = bf16[256,1536]{1,0:T(8,128)(2,1)S(1)} all-gather(bf16[256,384]{1,0:T(8,128)(2,1)S(1)} %fusion.90), channel_id=1, replica_groups=mesh['segment'=2,'blk'=32,'mp'=4] {'mp'}, dimensions={1}, use_global_device_ids=true | all-gather | bytes 983040 | tf_op jit(solution)/shard_map/all_gather | solution.py:100
  26.1 117.8 %all-gather.3.cloned.1.call-done = bf16[2,8192,384]{2,1,0:T(8,128)(2,1)} async-done(((bf16[2,256,384]{2,1,0:T(8,128)(2,1)}), bf16[2,8192,384]{2,1,0:T(8,128)(2,1)}) %all-gather.3.cloned.1.call-update) | async-done | bytes 12582928 | tf_op jit(solution)/shard_map/all_gather | solution.py:108
  143.9 10.2 %fusion.116 = (bf16[1,8192,384]{2,1,0:T(8,128)(2,1)}, bf16[1,8192,384]{2,1,0:T(8,128)(2,1)}) fusion(bf16[2,8192,384]{2,1,0:T(8,128)(2,1)} %all-gather.3.cloned.1.call-done), kind=kLoop, calls=%fused_computation.111 | loop fusion | bytes 25165824 | tf_op jit(solution)/shard_map/slice | solution.py:36
  154.1 16.6 %reshape.48 = bf16[8,1024,3,128]{3,2,1,0:T(4,128)(2,1)} reshape(bf16[1,8192,384]{2,1,0:T(8,128)(2,1)} %get-tuple-element.214) | data formatting | bytes 12582912 | tf_op jit(solution)/shard_map/reshape;squeeze | solution.py:35
  170.8 7.7 %copy.38 = bf16[8,1024,3,128]{3,1,2,0:T(8,128)(2,1)} copy(bf16[8,1024,3,128]{3,2,1,0:T(4,128)(2,1)} %reshape.48) | data formatting | bytes 12582912
  178.4 16.6 %reshape.49 = bf16[8,1024,3,128]{3,2,1,0:T(4,128)(2,1)} reshape(bf16[1,8192,384]{2,1,0:T(8,128)(2,1)} %get-tuple-element.213) | data formatting | bytes 12582912 | tf_op jit(solution)/shard_map/reshape;squeeze | solution.py:36
  195.1 13.0 %copy.40 = bf16[8,1024,3,128]{1,3,2,0:T(8,128)(2,1)} copy(bf16[8,1024,3,128]{3,2,1,0:T(4,128)(2,1)} %reshape.49) | data formatting | bytes 12582912
  208.1 65.1 %while.30 = (s32[]{:T(128)}, f32[256,3]{0,1:T(4,128)S(1)}, f32[256,3]{0,1:T(4,128)S(1)}, f32[256,3,128]{0,2,1:T(8,128)S(1)}, bf16[8,1024,3,128]{3,1,2,0:T(8,128)...) while((s32[]{:T(128)}, f32[256,3]{0,1:T(4,128)S(1)}, ...), condition=%wide.region_4.5_spmd.clone, body=%wide.region_1.4_spmd.clone.sunk | while | flops 409243392 | bytes 24626308 | solution.py:57
  216.2 3.4 bitcast_reduce_fusion.4
  224.4 3.4 bitcast_reduce_fusion.4
  232.5 3.4 bitcast_reduce_fusion.4
  248.8 3.4 bitcast_reduce_fusion.4
  256.9 3.4 bitcast_reduce_fusion.4
  265.0 3.4 bitcast_reduce_fusion.4
  275.1 20.2 %reduce-scatter.7.cloned.1.call-done = bf16[384,256]{1,0:T(8,128)(2,1)} async-done(((bf16[1536,256]{1,0:T(8,128)(2,1)}), bf16[384,256]{1,0:T(8,128)(2,1)}) %reduce-scatter.7.cloned.1.call-update) | async-done | bytes 196624
  296.4 4.5 collective-permute-start
  300.9 4.1 collective-permute-done
  305.0 8.7 %all_gather.17 = bf16[256,1536]{1,0:T(8,128)(2,1)S(1)} all-gather(bf16[256,384]{1,0:T(8,128)(2,1)S(1)} %collective-permute-done), channel_id=1, replica_groups=mesh['segment'=2,'blk'=32,'mp'=4] {'mp'}, dimensions={1}, use_global_device_ids=true | all-gather | bytes 983040 | tf_op jit(solution)/shard_map/all_gather | solution.py:119
  318.7 8.9 %all_gather.19 = bf16[256,1536]{1,0:T(8,128)(2,1)S(1)} all-gather(bf16[256,384]{1,0:T(8,128)(2,1)S(1)} %add_convert_fusion.1), channel_id=1, replica_groups=mesh['segment'=2,'blk'=32,'mp'=4] {'mp'}, dimensions={1}, use_global_device_ids=true | all-gather | bytes 983040 | tf_op jit(solution)/shard_map/all_gather | solution.py:115
  330.0 108.6 %all-gather.5.cloned.1.call-done = bf16[2,8192,384]{2,1,0:T(8,128)(2,1)} async-done(((bf16[2,256,384]{2,1,0:T(8,128)(2,1)}), bf16[2,8192,384]{2,1,0:T(8,128)(2,1)}) %all-gather.5.cloned.1.call-update) | async-done | bytes 12582928 | tf_op jit(solution)/shard_map/all_gather | solution.py:122
  438.6 10.2 %fusion.115 = (bf16[1,8192,384]{2,1,0:T(8,128)(2,1)}, bf16[1,8192,384]{2,1,0:T(8,128)(2,1)}) fusion(bf16[2,8192,384]{2,1,0:T(8,128)(2,1)} %all-gather.5.cloned.1.call-done), kind=kLoop, calls=%fused_computation.110 | loop fusion | bytes 25165824 | tf_op jit(solution)/shard_map/slice | solution.py:36
  448.8 16.6 %reshape.50 = bf16[8,1024,3,128]{3,2,1,0:T(4,128)(2,1)} reshape(bf16[1,8192,384]{2,1,0:T(8,128)(2,1)} %get-tuple-element.212) | data formatting | bytes 12582912 | tf_op jit(solution)/shard_map/reshape;squeeze | solution.py:35
  465.5 7.7 %copy.44 = bf16[8,1024,3,128]{3,1,2,0:T(8,128)(2,1)} copy(bf16[8,1024,3,128]{3,2,1,0:T(4,128)(2,1)} %reshape.50) | data formatting | bytes 12582912
  473.1 16.6 %reshape.51 = bf16[8,1024,3,128]{3,2,1,0:T(4,128)(2,1)} reshape(bf16[1,8192,384]{2,1,0:T(8,128)(2,1)} %get-tuple-element.211) | data formatting | bytes 12582912 | tf_op jit(solution)/shard_map/reshape;squeeze | solution.py:36
  489.8 13.0 %copy.46 = bf16[8,1024,3,128]{1,3,2,0:T(8,128)(2,1)} copy(bf16[8,1024,3,128]{3,2,1,0:T(4,128)(2,1)} %reshape.51) | data formatting | bytes 12582912
  502.8 65.2 %while.31 = (s32[]{:T(128)}, f32[256,3]{0,1:T(4,128)S(1)}, f32[256,3]{0,1:T(4,128)S(1)}, f32[256,3,128]{0,2,1:T(8,128)S(1)}, bf16[8,1024,3,128]{3,1,2,0:T(8,128)...) while((s32[]{:T(128)}, f32[256,3]{0,1:T(4,128)S(1)}, ...), condition=%wide.region_11.12_spmd.clone, body=%wide.region_8.11_spmd.clone.sunk | while | flops 409243392 | bytes 24626308 | solution.py:57
  502.8 3.5 bitcast_reduce_fusion.5
  519.2 3.4 bitcast_reduce_fusion.5
  527.3 3.4 bitcast_reduce_fusion.5
  535.5 3.4 bitcast_reduce_fusion.5
  543.6 3.4 bitcast_reduce_fusion.5
  569.8 20.4 %reduce-scatter.9.cloned.1.call-done = bf16[384,256]{1,0:T(8,128)(2,1)} async-done(((bf16[1536,256]{1,0:T(8,128)(2,1)}), bf16[384,256]{1,0:T(8,128)(2,1)}) %reduce-scatter.9.cloned.1.call-update) | async-done | bytes 196624
  (171 shorter events, 115.5 us)
Async XLA Ops:
  6.5 266.7 %copy-start = (bf16[1,384,1536]{2,1,0:T(8,128)(2,1)S(1)}, bf16[1,384,1536]{2,1,0:T(8,128)(2,1)}, u32[]{:S(2)}) copy-start(bf16[1,384,1536]{2,1,0:T(8,128)(2,1)} %param.19) | copy-start | bytes 3538948
  6.5 137.4 %all-gather.3.cloned.1.call-start = ((), (), s32[]{:S(2)}) async-start(), calls=%async_computation.2 | async-start | bytes 12976128 | tf_op jit(solution)/shard_map/all_gather | solution.py:108
  23.8 271.5 %reduce-scatter.7.cloned.1.call-start = ((), (), s32[]{:S(2)}) async-start(), calls=%async_computation.4 | async-start | bytes 983040
  211.5 2.8 copy-start.2
  219.6 2.8 copy-start.2
  227.8 2.8 copy-start.2
  235.9 2.8 copy-start.2
  244.0 2.8 copy-start.2
  252.2 2.8 copy-start.2
  260.3 2.8 copy-start.2
  268.4 2.8 copy-start.2
  273.2 40.8 %copy-start.5 = (f32[1536]{0:T(1024)S(1)}, f32[1536]{0:T(1024)}, u32[]{:S(2)}) copy-start(f32[1536]{0:T(1024)} %param.21) | copy-start | bytes 18436
  275.0 163.6 %all-gather.5.cloned.1.call-start = ((), (), s32[]{:S(2)}) async-start(), calls=%async_computation.3 | async-start | bytes 12976128 | tf_op jit(solution)/shard_map/all_gather | solution.py:122
  296.4 8.6 %collective-permute-start = (bf16[256,384]{1,0:T(8,128)(2,1)S(1)}, bf16[256,384]{1,0:T(8,128)(2,1)S(1)}, u32[]{:S(2)}, u32[]{:S(2)}) collective-permute-start(bf16[256,384]{1,0:T(8,128)(2,1)S(1)} %add_convert_fusion.1), channel_id=1, source_target_pairs={{0,128},{1,129},{2,130},{3,131},{4,132},{5,133},{6,134},{7,135},{8... | collective-permute-start | bytes 589832 | tf_op jit(solution)/shard_map/ppermute | solution.py:13
  315.9 11.9 %copy-start.6 = (f32[1536]{0:T(1024)S(1)}, f32[1536]{0:T(1024)}, u32[]{:S(2)}) copy-start(f32[1536]{0:T(1024)} %param.20) | copy-start | bytes 18436
  318.6 271.6 %reduce-scatter.9.cloned.1.call-start = ((), (), s32[]{:S(2)}) async-start(), calls=%async_computation.5 | async-start | bytes 983040
  502.8 65.2 %copy-start.4 = (bf16[384,1536]{1,0:T(8,128)(2,1)S(1)}, bf16[384,1536]{1,0:T(8,128)(2,1)}, u32[]{:S(2)}) copy-start(bf16[384,1536]{1,0:T(8,128)(2,1)} %param.23) | copy-start | bytes 3538948
  506.3 2.8 copy-start.3
  514.4 2.8 copy-start.3
  522.6 2.8 copy-start.3
  530.7 2.8 copy-start.3
  538.8 2.8 copy-start.3
  547.0 2.8 copy-start.3
  555.1 2.8 copy-start.3
  563.2 2.8 copy-start.3
  568.0 24.1 %copy-start.1 = (bf16[1,384,1536]{2,1,0:T(8,128)(2,1)S(1)}, bf16[1,384,1536]{2,1,0:T(8,128)(2,1)}, u32[]{:S(2)}) copy-start(bf16[1,384,1536]{2,1,0:T(8,128)(2,1)} %param.19) | copy-start | bytes 3538948
Sparse Core Ops, SparseCore 0:
  23.9 119.9 all-gather.2
  275.1 20.1 reduce-scatter.6
  318.7 119.8 all-gather.4
  569.9 20.2 reduce-scatter.8
where the time goes:
time: 603 us; the launch traced here: 599 us
  waiting for transfers between devices  271 us (45%)
  local copies, waits for them, and re-layouts  137 us (23%)
  matrix products  98.3 us (16%)
  other arithmetic  45.4 us (8%)
  blocking collectives  27.8 us (5%)
  between operations  13.4 us (2%)
    all_gather x1, waiting for transfers between devices, on_device(): lax.all_gather(self_pairs, 'blk', axis=1, tiled=True)  118 us
    all_gather x1, waiting for transfers between devices, on_device(): lax.all_gather(memory_pairs, 'blk', axis=1, tiled=True)  109 us
    dot_general x16, matrix products, absorb(): jnp.einsum('qhd,khd->qhk', grouped, key_block, preferred_element_type=jnp...  54.2 us
    unnamed x20, local copies, waits for them, and re-layouts  46.3 us
    reduce_sum x16, other arithmetic, absorb(): new_sum = running_sum * shrink + jnp.sum(weights, axis=2)  41.1 us
    unnamed x6, waiting for transfers between devices  40.7 us
    another operation x2, local copies, waits for them, and re-layouts, fold(): piece[0].reshape(piece_rows // block_rows, block_rows, head_count, HEAD_DIM)  33.3 us
    another operation x2, local copies, waits for them, and re-layouts, fold(): piece[1].reshape(piece_rows // block_rows, block_rows, head_count, HEAD_DIM)  33.3 us
  transfers between devices with their start and end apart: 5, of which 5 were waited for; matrix products, arithmetic and copies ran while one was open for 1% of the time, Pallas kernels for 0%

commit v1 on v0

--- a/solution.py
+++ b/solution.py
@@ -1,3 +1,4 @@
+import functools
 import math
 import jax
 import jax.numpy as jnp
@@ -5,6 +6,21 @@
 from jax.sharding import PartitionSpec as P
 
 HEAD_DIM = 128
+
+
+def attach_joints_in(u, net_axis, join_dim):
+    return jnp.concatenate(
+        lax.all_to_all(
+            jnp.stack([u for _ in range(lax.axis_size(net_axis))], axis=0),
+            axis_name=net_axis,
+            split_axis=0,
+            concat_axis=0,
+        ),
+        axis=join_dim,
+    )
+
+
+finish_copies = functools.partial(attach_joints_in, net_axis="blk", join_dim=1)
 
 
 def shifted(value, axis, steps):
@@ -104,9 +120,7 @@
         [project(normed, self_weights[0, 1]), project(normed, self_weights[0, 2])]
     )
     fold_self, self_start = make_fold(self_queries)
-    self_running = fold_self(
-        self_start, lax.all_gather(self_pairs, "blk", axis=1, tiled=True), jnp.int32(0)
-    )
+    self_running = fold_self(self_start, finish_copies(self_pairs), jnp.int32(0))
     partial_out = jnp.dot(finish(self_running), self_out[0], preferred_element_type=jnp.float32)
     reduced = lax.psum_scatter(
         partial_out.astype(jnp.bfloat16), "mp", scatter_dimension=1, tiled=True

time: 603 us -> 803 us (1.33)
  waiting for transfers between devices: 271 us -> 457 us
  starting transfers between devices: 4.58 us -> 15.5 us
    all_to_all x0 -> x1, waiting for transfers between devices: none -> 287 us  [attach_joints_in(): lax.all_to_all(jnp.stack([u for _ in range(lax.axis_size(net_axis))], axi...]
    all_gather x1 -> x0, waiting for transfers between devices: 118 us -> none  [on_device(): lax.all_gather(self_pairs, 'blk', axis=1, tiled=True)]
    unnamed x6 -> x5, waiting for transfers between devices: 40.7 us -> 56.9 us
    all_to_all x0 -> x1, starting transfers between devices: none -> 10.9 us  [attach_joints_in(): lax.all_to_all(jnp.stack([u for _ in range(lax.axis_size(net_axis))], axi...]
    slice x2 -> x3, local copies, waits for them, and re-layouts: 20.4 us -> 27.4 us  [fold(): piece[1].reshape(piece_rows // block_rows, block_rows, head_count, HEAD_DIM)]
where the time goes in v1:
time: 803 us; the launch traced here: 799 us
  waiting for transfers between devices  457 us (57%)
  local copies, waits for them, and re-layouts  143 us (18%)
  matrix products  98.3 us (12%)
  other arithmetic  44.6 us (6%)
  blocking collectives  27.7 us (3%)
  starting transfers between devices  15.5 us (2%)
  between operations  13.4 us (2%)
    all_to_all x1, waiting for transfers between devices, attach_joints_in(): lax.all_to_all(jnp.stack([u for _ in range(lax.axis_size(net_axis))], axi...  287 us
    all_gather x1, waiting for transfers between devices, on_device(): lax.all_gather(memory_pairs, 'blk', axis=1, tiled=True)  109 us
    unnamed x5, waiting for transfers between devices  56.9 us
    dot_general x16, matrix products, absorb(): jnp.einsum('qhd,khd->qhk', grouped, key_block, preferred_element_type=jnp...  54.2 us
    unnamed x20, local copies, waits for them, and re-layouts  43.6 us
    reduce_sum x16, other arithmetic, absorb(): new_sum = running_sum * shrink + jnp.sum(weights, axis=2)  41.1 us
    dot_general x16, matrix products, absorb(): jnp.einsum('qhk,khd->qhd', weights.astype(jnp.bfloat16), value_block, pre...  30.2 us
    slice x3, local copies, waits for them, and re-layouts, fold(): piece[1].reshape(piece_rows // block_rows, block_rows, head_count, HEAD_DIM)  27.4 us
  transfers between devices with their start and end apart: 5, of which 5 were waited for; matrix products, arithmetic and copies ran while one was open for 1% of the time, Pallas kernels for 0%

profile of v1, /device:TPU:1, one launch (start us, length us, event | category | flops | bytes accessed | tf_op | source)
XLA Modules:
  0.0 799.2 jit_solution(14679531631344974068)
XLA Ops:
  8.0 10.3 %all_gather.12 = bf16[256,1536]{1,0:T(8,128)(2,1)S(1)} all-gather(bf16[256,384]{1,0:T(8,128)(2,1)S(1)} %fusion.90), channel_id=1, replica_groups=mesh['segment'=2,'blk'=32,'mp'=4] {'mp'}, dimensions={1}, use_global_device_ids=true | all-gather | bytes 983040 | tf_op jit(solution)/shard_map/all_gather | solution.py:116
  23.2 6.1 stack.17
  29.3 10.9 %all-to-all-start = ((bf16[32,2,256,384]{2,3,1,0:T(8,128)(2,1)}), bf16[32,2,256,384]{2,3,1,0:T(8,128)(2,1)}, u32[]{:S(2)}, u32[]{:S(2)}) async-start(bf16[32,2,256,384]{2,3,1,0:T(8,128)(2,1)} %stack.17), calls=%async_computation | async-start | bytes 25165824 | tf_op jit(solution)/shard_map/all_to_all | solution.py:13
  42.7 286.9 %all-to-all-done = bf16[32,2,256,384]{2,3,1,0:T(8,128)(2,1)} async-done(((bf16[32,2,256,384]{2,3,1,0:T(8,128)(2,1)}), bf16[32,2,256,384]{2,3,1,0:T(8,128)(2,1)}, u32[]{:S(2)}, u32[]{:S(2)}) %all-to-all-start) | async-done | bytes 12582944 | tf_op jit(solution)/shard_map/all_to_all | solution.py:13
  329.6 8.3 %fusion.116 = (bf16[1,32,256,384]{2,3,0,1:T(8,128)(2,1)}, bf16[1,32,256,384]{2,3,0,1:T(8,128)(2,1)S(1)}) fusion(bf16[2,32,256,384]{2,3,0,1:T(8,128)(2,1)} %bitcast.7), kind=kLoop, calls=%fused_computation.111 | loop fusion | bytes 25165824 | tf_op jit(solution)/shard_map/slice | solution.py:52
  337.8 6.3 copy.33
  344.2 10.8 %reshape_squeeze.12 = bf16[8,1024,3,128]{1,0,3,2:T(8,128)(2,1)} reshape(bf16[1,32,256,384]{2,1,3,0:T(8,128)(2,1)} %copy.33) | data formatting | bytes 12582912 | tf_op jit(solution)/shard_map/reshape;squeeze | solution.py:51
  354.9 9.1 %copy.36 = bf16[8,1024,3,128]{3,1,2,0:T(8,128)(2,1)} copy(bf16[8,1024,3,128]{1,0,3,2:T(8,128)(2,1)} %reshape_squeeze.12) | data formatting | bytes 12582912
  364.1 9.0 %copy.35 = bf16[1,32,256,384]{2,1,3,0:T(8,128)(2,1)} copy(bf16[1,32,256,384]{2,3,0,1:T(8,128)(2,1)} %get-tuple-element.213) | data formatting | bytes 12582912 | tf_op jit(solution)/shard_map/slice | solution.py:52
  373.0 10.7 %reshape_squeeze.13 = bf16[8,1024,3,128]{1,0,3,2:T(8,128)(2,1)} reshape(bf16[1,32,256,384]{2,1,3,0:T(8,128)(2,1)} %copy.35) | data formatting | bytes 12582912 | tf_op jit(solution)/shard_map/reshape;squeeze | solution.py:52
  383.7 8.9 %copy.38 = bf16[8,1024,3,128]{1,3,2,0:T(8,128)(2,1)} copy(bf16[8,1024,3,128]{1,0,3,2:T(8,128)(2,1)} %reshape_squeeze.13) | data formatting | bytes 12582912
  392.7 65.1 %while.30 = (s32[]{:T(128)}, f32[256,3]{0,1:T(4,128)S(1)}, f32[256,3]{0,1:T(4,128)S(1)}, f32[256,3,128]{0,2,1:T(8,128)S(1)}, bf16[8,1024,3,128]{3,1,2,0:T(8,128)...) while((s32[]{:T(128)}, f32[256,3]{0,1:T(4,128)S(1)}, ...), condition=%wide.region_4.5_spmd.clone, body=%wide.region_1.4_spmd.clone.sunk | while | flops 409243392 | bytes 24626308 | solution.py:73
  400.8 3.4 bitcast_reduce_fusion.4
  408.9 3.4 bitcast_reduce_fusion.4
  417.1 3.4 bitcast_reduce_fusion.4
  425.2 3.4 bitcast_reduce_fusion.4
  433.4 3.4 bitcast_reduce_fusion.4
  441.5 3.4 bitcast_reduce_fusion.4
  459.6 36.4 %reduce-scatter.7.cloned.1.call-done = bf16[384,256]{1,0:T(8,128)(2,1)} async-done(((bf16[1536,256]{1,0:T(8,128)(2,1)}), bf16[384,256]{1,0:T(8,128)(2,1)}) %reduce-scatter.7.cloned.1.call-update) | async-done | bytes 196624
  497.2 4.3 collective-permute-start
  501.5 4.1 collective-permute-done
  505.6 8.7 %all_gather.13 = bf16[256,1536]{1,0:T(8,128)(2,1)S(1)} all-gather(bf16[256,384]{1,0:T(8,128)(2,1)S(1)} %collective-permute-done), channel_id=1, replica_groups=mesh['segment'=2,'blk'=32,'mp'=4] {'mp'}, dimensions={1}, use_global_device_ids=true | all-gather | bytes 983040 | tf_op jit(solution)/shard_map/all_gather | solution.py:133
  519.2 8.7 %all_gather.15 = bf16[256,1536]{1,0:T(8,128)(2,1)S(1)} all-gather(bf16[256,384]{1,0:T(8,128)(2,1)S(1)} %add_convert_fusion.1), channel_id=1, replica_groups=mesh['segment'=2,'blk'=32,'mp'=4] {'mp'}, dimensions={1}, use_global_device_ids=true | all-gather | bytes 983040 | tf_op jit(solution)/shard_map/all_gather | solution.py:129
  530.4 108.8 %all-gather.2.cloned.1.call-done = bf16[2,8192,384]{2,1,0:T(8,128)(2,1)} async-done(((bf16[2,256,384]{2,1,0:T(8,128)(2,1)}), bf16[2,8192,384]{2,1,0:T(8,128)(2,1)}) %all-gather.2.cloned.1.call-update) | async-done | bytes 12582928 | tf_op jit(solution)/shard_map/all_gather | solution.py:136
  639.2 10.2 %fusion.115 = (bf16[1,8192,384]{2,1,0:T(8,128)(2,1)}, bf16[1,8192,384]{2,1,0:T(8,128)(2,1)}) fusion(bf16[2,8192,384]{2,1,0:T(8,128)(2,1)} %all-gather.2.cloned.1.call-done), kind=kLoop, calls=%fused_computation.110 | loop fusion | bytes 25165824 | tf_op jit(solution)/shard_map/slice | solution.py:52
  649.4 16.6 %reshape.59 = bf16[8,1024,3,128]{3,2,1,0:T(4,128)(2,1)} reshape(bf16[1,8192,384]{2,1,0:T(8,128)(2,1)} %get-tuple-element.212) | data formatting | bytes 12582912 | tf_op jit(solution)/shard_map/reshape;squeeze | solution.py:51
  666.0 7.7 copy.42
  673.7 16.6 %reshape.60 = bf16[8,1024,3,128]{3,2,1,0:T(4,128)(2,1)} reshape(bf16[1,8192,384]{2,1,0:T(8,128)(2,1)} %get-tuple-element.211) | data formatting | bytes 12582912 | tf_op jit(solution)/shard_map/reshape;squeeze | solution.py:52
  690.3 13.0 %copy.44 = bf16[8,1024,3,128]{1,3,2,0:T(8,128)(2,1)} copy(bf16[8,1024,3,128]{3,2,1,0:T(4,128)(2,1)} %reshape.60) | data formatting | bytes 12582912
  703.4 65.2 %while.31 = (s32[]{:T(128)}, f32[256,3]{0,1:T(4,128)S(1)}, f32[256,3]{0,1:T(4,128)S(1)}, f32[256,3,128]{0,2,1:T(8,128)S(1)}, bf16[8,1024,3,128]{3,1,2,0:T(8,128)...) while((s32[]{:T(128)}, f32[256,3]{0,1:T(4,128)S(1)}, ...), condition=%wide.region_11.12_spmd.clone, body=%wide.region_8.11_spmd.clone.sunk | while | flops 409243392 | bytes 24626308 | solution.py:73
  703.4 3.5 bitcast_reduce_fusion.5
  770.4 20.4 %reduce-scatter.9.cloned.1.call-done = bf16[384,256]{1,0:T(8,128)(2,1)} async-done(((bf16[1536,256]{1,0:T(8,128)(2,1)}), bf16[384,256]{1,0:T(8,128)(2,1)}) %reduce-scatter.9.cloned.1.call-update) | async-done | bytes 196624
  (174 shorter events, 128.6 us)
Async XLA Ops:
  6.5 451.3 %copy-start = (bf16[1,384,1536]{2,1,0:T(8,128)(2,1)S(1)}, bf16[1,384,1536]{2,1,0:T(8,128)(2,1)}, u32[]{:S(2)}) copy-start(bf16[1,384,1536]{2,1,0:T(8,128)(2,1)} %param.19) | copy-start | bytes 3538948
  29.3 300.3 %all-to-all-start = ((bf16[32,2,256,384]{2,3,1,0:T(8,128)(2,1)}), bf16[32,2,256,384]{2,3,1,0:T(8,128)(2,1)}, u32[]{:S(2)}, u32[]{:S(2)}) async-start(bf16[32,2,256,384]{2,3,1,0:T(8,128)(2,1)} %stack.17), calls=%async_computation | async-start | bytes 25165824 | tf_op jit(solution)/shard_map/all_to_all | solution.py:13
  40.2 455.9 %reduce-scatter.7.cloned.1.call-start = ((), (), s32[]{:S(2)}) async-start(), calls=%async_computation.4 | async-start | bytes 983040
  396.1 2.8 copy-start.2
  404.2 2.8 copy-start.2
  412.3 2.8 copy-start.2
  420.5 2.8 copy-start.2
  428.6 2.8 copy-start.2
  436.7 2.8 copy-start.2
  444.9 2.8 copy-start.2
  453.0 2.8 copy-start.2
  457.8 56.7 %copy-start.5 = (f32[1536]{0:T(1024)S(1)}, f32[1536]{0:T(1024)}, u32[]{:S(2)}) copy-start(f32[1536]{0:T(1024)} %param.21) | copy-start | bytes 18436
  459.6 179.6 %all-gather.2.cloned.1.call-start = ((), (), s32[]{:S(2)}) async-start(), calls=%async_computation.3 | async-start | bytes 12976128 | tf_op jit(solution)/shard_map/all_gather | solution.py:136
  497.2 8.3 %collective-permute-start = (bf16[256,384]{1,0:T(8,128)(2,1)S(1)}, bf16[256,384]{1,0:T(8,128)(2,1)S(1)}, u32[]{:S(2)}, u32[]{:S(2)}) collective-permute-start(bf16[256,384]{1,0:T(8,128)(2,1)S(1)} %add_convert_fusion.1), channel_id=1, source_target_pairs={{0,128},{1,129},{2,130},{3,131},{4,132},{5,133},{6,134},{7,135},{8... | collective-permute-start | bytes 589832 | tf_op jit(solution)/shard_map/ppermute | solution.py:29
  516.4 11.8 %copy-start.6 = (f32[1536]{0:T(1024)S(1)}, f32[1536]{0:T(1024)}, u32[]{:S(2)}) copy-start(f32[1536]{0:T(1024)} %param.20) | copy-start | bytes 18436
  519.1 271.7 %reduce-scatter.9.cloned.1.call-start = ((), (), s32[]{:S(2)}) async-start(), calls=%async_computation.5 | async-start | bytes 983040
  703.4 65.2 %copy-start.4 = (bf16[384,1536]{1,0:T(8,128)(2,1)S(1)}, bf16[384,1536]{1,0:T(8,128)(2,1)}, u32[]{:S(2)}) copy-start(bf16[384,1536]{1,0:T(8,128)(2,1)} %param.23) | copy-start | bytes 3538948
  706.9 2.8 copy-start.3
  715.0 2.8 copy-start.3
  723.1 2.8 copy-start.3
  731.3 2.8 copy-start.3
  739.4 2.8 copy-start.3
  747.5 2.8 copy-start.3
  755.7 2.8 copy-start.3
  763.8 2.8 copy-start.3
  768.6 24.1 %copy-start.1 = (bf16[1,384,1536]{2,1,0:T(8,128)(2,1)S(1)}, bf16[1,384,1536]{2,1,0:T(8,128)(2,1)}, u32[]{:S(2)}) copy-start(bf16[1,384,1536]{2,1,0:T(8,128)(2,1)} %param.19) | copy-start | bytes 3538948
Sparse Core Ops, SparseCore 0:
  459.7 36.3 reduce-scatter.6
  519.2 119.9 all-gather.1
  770.5 20.2 reduce-scatter.8
